TPU v7x, 128 devices: a whole 4x4x4 slice. The times are simulated.
128 devices in a mesh: col: 8 (over z, core), grp: 16 (over x, y).
Axes of the slice: x: 4, y: 4, z: 4, core: 2. Of those that a mesh axis runs over, the one named last changes fastest.
Arguments:
- factor_rows: float32 [1024, 4, 8, 512], P('grp', None, 'col'), may hold values from -3 to 3, as said below
- new_rows: float32 [8192, 4, 8, 512], P('grp', None, 'col'), may hold values from -0.3125 to 0.3125
Outputs:
- updated_rows: float32 [1024, 4, 8, 512], P('grp', None, 'col')
Inputs may be any that keep to these rules, and one draw needn't show every extreme that they name: factor_rows is upper triangular in the global row and column numbers, with diagonal entries between 1 and 3.
All inputs are finite; a program needn't handle non-finite values.
Results may differ from a plain program's by a relative error of at most 0.00008.
Values sent between devices are 32-bit elements; how exact they have to be, the bound alone decides.
No kernel may reach another device: no remote copies, remote signals or barrier semaphores. Data moves between devices by JAX's collectives and lax.ppermute only.
A program may use at most 128 MiB of HBM per device.

v0:
```python
import jax
import jax.numpy as jnp
from jax import lax
from jax.sharding import PartitionSpec as P


def from_root(value, axis, source):
    kept = jnp.where(lax.axis_index(axis) == source, value, 0).astype(value.dtype)
    return lax.psum(kept, axis)


def solve_lower(lower, right):
    return lax.linalg.triangular_solve(lower, right, left_side=True, lower=True)


def shards(factor_rows, new_rows):
    highest = lax.Precision.HIGHEST
    own_rows = factor_rows.shape[0]
    npanel = factor_rows.shape[1]
    width = factor_rows.shape[3]
    local = jnp.concatenate([factor_rows, new_rows], 0).reshape(-1, npanel * width)
    panel = local[:, :width]
    first = from_root(panel, "col", 0)
    second = from_root(panel, "col", 1)
    part_one = jnp.dot(first.T, local, precision=highest, preferred_element_type=jnp.float32)
    part_two = jnp.dot(second.T, local, precision=highest, preferred_element_type=jnp.float32)
    both = jnp.concatenate([first, second], 1)
    small_one = jnp.dot(first.T, both, precision=highest, preferred_element_type=jnp.float32)
    small_two = jnp.dot(second.T, second, precision=highest, preferred_element_type=jnp.float32)
    gram_one, gram_two, corner_one, corner_two = lax.psum(
        (part_one, part_two, small_one, small_two), "grp"
    )
    lower_one = jnp.linalg.cholesky(corner_one[:, :width])
    cross = solve_lower(lower_one, corner_one[:, width:])
    lower_two = jnp.linalg.cholesky(corner_two - jnp.dot(cross.T, cross, precision=highest))
    upper_one = solve_lower(lower_one, gram_one)
    upper_two = solve_lower(lower_two, gram_two - jnp.dot(cross.T, upper_one, precision=highest))
    stacked = jnp.concatenate([upper_one, upper_two], 0)
    mine = lax.dynamic_slice_in_dim(stacked, lax.axis_index("grp") * own_rows, own_rows, 0)
    return mine.reshape(own_rows, npanel, 1, width)


def solution(mesh):
    placed = (P("grp", None, "col", None), P("grp", None, "col", None))
    return jax.shard_map(
        shards, mesh=mesh, in_specs=placed, out_specs=P("grp", None, "col", None), check_vma=False
    )
```

profile of v0, /device:TPU:1, one launch (start us, length us, event | category | flops | bytes accessed | tf_op | source)
XLA Modules:
  0.0 635.1 jit_solution(15138732121004060162)
XLA Ops:
  6.5 15.4 %maximum_reduce_fusion = f32[576,4,512]{2,1,0:T(4,128)S(1)} fusion(f32[512,4,1,512]{3,2,1,0:T(1,128)} %param.6, f32[64,4,1,512]{3,2,1,0:T(1,128)} %param.5), kind=kLoop, calls=%fused_computation.12 | loop fusion | flops 1179648 | bytes 9437184 | tf_op jit(solution)/shard_map/concatenate | solution.py:21
  22.0 4.3 copy.11
  26.3 3.1 slice_select_fusion.1
  29.9 68.0 %all-reduce.8.cloned.1.call-done = (f32[576,512]{1,0:T(8,128)}, f32[576,512]{1,0:T(8,128)}) async-done(((f32[576,512]{1,0:T(8,128)}, f32[576,512]{1,0:T(8,128)}), (f32[576,512]{1,0:T(8,128)}, f32[576,512]{1,0:T(8,128)})) %all-reduce.8.cloned.1.call-update) | async-done | bytes 2359312 | tf_op jit(solution)/shard_map/psum | solution.py:9
  97.9 13.7 %fusion.115 = f32[512,2048]{1,0:T(8,128)} fusion(f32[576,512]{1,0:T(8,128)} %get-tuple-element.51, f32[576,2048]{1,0:T(8,128)} %bitcast.121), kind=kOutput, calls=%fused_computation.189 | convolution fusion | flops 7247757312 | bytes 10092544 | tf_op jit(solution)/shard_map/dot_general | solution.py:26
  111.7 6.5 %fusion.29 = f32[512,1024]{0,1:T(8,128)} fusion(f32[576,512]{1,0:T(8,128)S(1)} %copy-done.1, f32[576,512]{1,0:T(8,128)S(1)} %copy-done), kind=kOutput, calls=%fused_computation.40 | convolution fusion | flops 3624468480 | bytes 4456448 | tf_op jit(solution)/shard_map/dot_general | solution.py:28
  118.2 11.9 %fusion.113 = f32[512,2048]{1,0:T(8,128)} fusion(f32[576,512]{1,0:T(8,128)S(1)} %copy-done.1, f32[576,2048]{1,0:T(8,128)S(1)} %bitcast.124), kind=kOutput, calls=%fused_computation.187 | convolution fusion | flops 7247757312 | bytes 10092544 | tf_op jit(solution)/shard_map/dot_general | solution.py:25
  130.0 3.8 fusion.114
  133.8 169.6 %all-reduce.6.cloned.1.call-done = (f32[512,2048]{1,0:T(8,128)}, f32[512,2048]{1,0:T(8,128)}, f32[512,1024]{0,1:T(8,128)}, f32[512,512]{0,1:T(8,128)}) async-done(((f32[512,2048]{1,0:T(8,128)}, f32[512,2048]{1,0:T(8,128)}, f32[512,1024]{0,1:T(8,128)}, f32[512,512]{0,1:T(8,128)}), (f32[512,2048]{1,0:T(8,128)}, f32[512,2048]{1,0:T(8,128)}, f32[512,1024]{0,1:T(8,128)}, ...) | async-done | bytes 11534352 | tf_op jit(solution)/shard_map/psum | solution.py:30
  303.4 2.4 slice.184
  305.8 1.6 copy.4
  307.6 1.1 copy-done.6
  308.7 11.7 %cholesky.286 = f32[128,128]{1,0:T(8,128)S(1)} custom-call(f32[128,128]{1,0:T(8,128)S(1)} %cholesky.426), custom_call_target="Cholesky" | custom-call | tf_op jit(solution)/shard_map/jit(cholesky)/cholesky | solution.py:33
  320.6 9.8 %custom-call.31 = f32[1,128,128]{1,2,0:T(8,128)S(1)} custom-call(f32[1,128,128]{2,1,0:T(8,128)S(1)} %get-tuple-element.78), custom_call_target="InvertDiagBlocksLowerTriangular" | custom-call | tf_op jit(solution)/shard_map/jit(cholesky)/cholesky | solution.py:33
  330.4 1.2 constant_dynamic-update-slice_fusion.1
  331.6 1.3 convolution_subtract_fusion.9
  332.9 12.1 %cholesky.305 = f32[128,128]{1,0:T(8,128)S(1)} custom-call(f32[128,128]{1,0:T(8,128)S(1)} %cholesky.430), custom_call_target="Cholesky" | custom-call | tf_op jit(solution)/shard_map/jit(cholesky)/cholesky | solution.py:33
  345.0 9.8 %custom-call.32 = f32[1,128,128]{1,2,0:T(8,128)S(1)} custom-call(f32[1,128,128]{2,1,0:T(8,128)S(1)} %get-tuple-element.75), custom_call_target="InvertDiagBlocksLowerTriangular" | custom-call | tf_op jit(solution)/shard_map/jit(cholesky)/cholesky | solution.py:33
  355.1 1.3 convolution_subtract_fusion.11
  356.4 11.7 %cholesky.326 = f32[128,128]{1,0:T(8,128)S(1)} custom-call(f32[128,128]{1,0:T(8,128)S(1)} %cholesky.435), custom_call_target="Cholesky" | custom-call | tf_op jit(solution)/shard_map/jit(cholesky)/cholesky | solution.py:33
  368.9 9.8 %custom-call.33 = f32[1,128,128]{1,2,0:T(8,128)S(1)} custom-call(f32[1,128,128]{2,1,0:T(8,128)S(1)} %get-tuple-element.72), custom_call_target="InvertDiagBlocksLowerTriangular" | custom-call | tf_op jit(solution)/shard_map/jit(cholesky)/cholesky | solution.py:33
  378.9 1.2 convolution_subtract_fusion.13
  380.1 11.9 %cholesky.343 = f32[128,128]{1,0:T(8,128)S(1)} custom-call(f32[128,128]{1,0:T(8,128)S(1)} %convolution_subtract_fusion.13), custom_call_target="Cholesky" | custom-call | tf_op jit(solution)/shard_map/jit(cholesky)/cholesky | solution.py:33
  395.9 1.2 select_select_fusion.1
  397.2 11.7 %while.5 = (s32[]{:T(128)}, f32[512,512]{1,0:T(8,128)}, s32[4,2]{0,1:T(2,128)S(1)}, f32[4,128,128]{2,1,0:T(8,128)S(1)}, s32[]{:T(128)}) while((s32[]{:T(128)}, f32[512,512]{1,0:T(8,128)}, s32[4,2]{0,1:T(2,128)S(1)}, f32[4,128,128]{2,1,0:T(8,128)S(1)}, s32[]{:T(128)}) %tuple.55), condition=%wide.while_cond, body=%wide.while_body.sunk | while | flops 2 | bytes 131181 | solution.py:13
  397.8 2.3 bitcast_dynamic-update-slice_fusion.4
  400.8 2.3 bitcast_dynamic-update-slice_fusion.4
  403.7 2.3 bitcast_dynamic-update-slice_fusion.4
  406.7 2.2 bitcast_dynamic-update-slice_fusion.4
  408.9 39.3 %custom-call.34 = f32[4,128,128]{1,2,0:T(8,128)S(1)} custom-call(f32[4,128,128]{2,1,0:T(8,128)S(1)} %get-tuple-element.29), custom_call_target="InvertDiagBlocksLowerTriangular" | custom-call | tf_op jit(solution)/shard_map/triangular_solve/custom-call.3 | solution.py:13
  448.7 1.4 convolution_subtract_fusion.6
  450.5 1.9 convolution_subtract_fusion.5
  452.9 2.4 convolution_subtract_fusion.7
  455.7 3.1 convolution_subtract_fusion.4
  460.4 11.7 %cholesky.358 = f32[128,128]{1,0:T(8,128)S(1)} custom-call(f32[128,128]{1,0:T(8,128)S(1)} %cholesky.439), custom_call_target="Cholesky" | custom-call | tf_op jit(solution)/shard_map/jit(cholesky)/cholesky | solution.py:35
  472.2 10.2 %custom-call.35 = f32[1,128,128]{1,2,0:T(8,128)S(1)} custom-call(f32[1,128,128]{2,1,0:T(8,128)S(1)} %get-tuple-element.68), custom_call_target="InvertDiagBlocksLowerTriangular" | custom-call | tf_op jit(solution)/shard_map/jit(cholesky)/cholesky | solution.py:35
  482.4 1.2 constant_dynamic-update-slice_fusion
  483.7 1.3 convolution_subtract_fusion.8
  484.9 11.7 %cholesky.377 = f32[128,128]{1,0:T(8,128)S(1)} custom-call(f32[128,128]{1,0:T(8,128)S(1)} %cholesky.443), custom_call_target="Cholesky" | custom-call | tf_op jit(solution)/shard_map/jit(cholesky)/cholesky | solution.py:35
  498.0 9.8 %custom-call.36 = f32[1,128,128]{1,2,0:T(8,128)S(1)} custom-call(f32[1,128,128]{2,1,0:T(8,128)S(1)} %get-tuple-element.65), custom_call_target="InvertDiagBlocksLowerTriangular" | custom-call | tf_op jit(solution)/shard_map/jit(cholesky)/cholesky | solution.py:35
  508.1 1.3 convolution_subtract_fusion.10
  509.4 11.7 %cholesky.398 = f32[128,128]{1,0:T(8,128)S(1)} custom-call(f32[128,128]{1,0:T(8,128)S(1)} %cholesky.448), custom_call_target="Cholesky" | custom-call | tf_op jit(solution)/shard_map/jit(cholesky)/cholesky | solution.py:35
  521.8 10.0 %custom-call.37 = f32[1,128,128]{1,2,0:T(8,128)S(1)} custom-call(f32[1,128,128]{2,1,0:T(8,128)S(1)} %get-tuple-element.62), custom_call_target="InvertDiagBlocksLowerTriangular" | custom-call | tf_op jit(solution)/shard_map/jit(cholesky)/cholesky | solution.py:35
  532.0 1.2 convolution_subtract_fusion.12
  533.2 11.7 %cholesky.415 = f32[128,128]{1,0:T(8,128)S(1)} custom-call(f32[128,128]{1,0:T(8,128)S(1)} %convolution_subtract_fusion.12), custom_call_target="Cholesky" | custom-call | tf_op jit(solution)/shard_map/jit(cholesky)/cholesky | solution.py:35
  548.4 8.3 %while.6 = (s32[]{:T(128)}, f32[512,512]{1,0:T(8,128)S(1)}, s32[4,2]{0,1:T(2,128)S(1)}, f32[4,128,128]{2,1,0:T(8,128)S(1)}, s32[]{:T(128)}) while((s32[]{:T(128)}, f32[512,512]{1,0:T(8,128)S(1)}, s32[4,2]{0,1:T(2,128)S(1)}, f32[4,128,128]{2,1,0:T(8,128)S(1)}, s32[]{:T(128)}) %tuple.67), condition=%wide.while_cond.clone, body=%wide.while_body.clone.sunk | while | flops 2 | bytes 131181 | solution.py:13
  549.0 1.4 bitcast_dynamic-update-slice_fusion.5
  551.1 1.4 bitcast_dynamic-update-slice_fusion.5
  553.2 1.4 bitcast_dynamic-update-slice_fusion.5
  555.3 1.4 bitcast_dynamic-update-slice_fusion.5
  556.7 39.5 %custom-call.38 = f32[4,128,128]{1,2,0:T(8,128)S(1)} custom-call(f32[4,128,128]{2,1,0:T(8,128)S(1)} %get-tuple-element.30), custom_call_target="InvertDiagBlocksLowerTriangular" | custom-call | tf_op jit(solution)/shard_map/triangular_solve/custom-call.3 | solution.py:13
  596.2 2.3 fusion.41
  598.5 2.4 convolution_subtract_fusion.3
  601.0 1.1 fusion.95
  602.0 2.2 convolution_subtract_fusion.1
  604.2 1.1 fusion.97
  605.3 3.1 fusion.26
  609.5 7.8 %fusion.20 = f32[512,2048]{1,0:T(8,128)S(1)} fusion(f32[512,2048]{1,0:T(8,128)S(1)} %copy-done.3, f32[128,2048]{1,0:T(8,128)S(1)} %fusion.99, f32[128,2048]{1,0:T(8,128)S(1)} %fusion.97, f32[128,2048]{1,0:T(8,128)S(1)} %fusion.95, f32[128,2048]{1,0:T(8,128)S(1)} %fusion.41, f32[128,512]{1,0:T(8,128)S(1)} %fusion.98, f32[128,512]{1,0:T(8,128)S(1)} %fusion.96, ...), kind=kOutput, calls=%fused_computation.33 | convolution fusion | flops 6447431680 | bytes 13631488 | tf_op jit(solution)/shard_map/dot_general | solution.py:37
  619.4 1.1 fusion.83
  620.4 1.3 convolution_subtract_fusion
  621.7 1.1 fusion.81
  622.7 2.0 fusion.23
  624.8 1.1 fusion.80
  626.4 1.4 reshape.50
  (85 shorter events, 19.5 us)
Async XLA Ops:
  6.5 91.4 %all-reduce.8.cloned.1.call-start = ((), (), s32[]{:S(2)}) async-start(), calls=%async_computation.1 | async-start | bytes 4718592 | tf_op jit(solution)/shard_map/psum | solution.py:9
  29.4 88.8 %slice-start = ((s8[4718592]{0:T(1024)(128)(4,1)}), s8[524288]{0:T(1024)(128)(4,1)S(1)}, s32[]{:S(2)}) async-start(s8[4718592]{0:T(1024)(128)(4,1)} %bitcast.122), calls=%async_computation.2 | async-start | bytes 1048576
  29.4 273.9 %all-reduce.6.cloned.1.call-start = ((), (), s32[]{:S(2)}) async-start(), calls=%async_computation | async-start | bytes 23068672 | tf_op jit(solution)/shard_map/psum | solution.py:30
  97.9 13.7 %copy-start = (f32[576,512]{1,0:T(8,128)S(1)}, f32[576,512]{1,0:T(8,128)}, u32[]{:S(2)}) copy-start(f32[576,512]{1,0:T(8,128)} %get-tuple-element.51) | copy-start | bytes 3538948
  97.9 13.8 %copy-start.1 = (f32[576,512]{1,0:T(8,128)S(1)}, f32[576,512]{1,0:T(8,128)}, u32[]{:S(2)}) copy-start(f32[576,512]{1,0:T(8,128)} %get-tuple-element.52) | copy-start | bytes 3538948
  97.9 20.2 %slice-start.1 = ((s8[4718592]{0:T(1024)(128)(4,1)}), s8[4194304]{0:T(1024)(128)(4,1)S(1)}, s32[]{:S(2)}) async-start(s8[4718592]{0:T(1024)(128)(4,1)} %bitcast.122), calls=%async_computation.3 | async-start | bytes 8388608
  303.4 4.0 copy-start.2
  307.6 1.1 copy-start.6
  448.2 7.5 %copy-start.7 = (f32[4,128,128]{1,2,0:T(8,128)}, f32[4,128,128]{1,2,0:T(8,128)S(1)}, u32[]{:S(2)}) copy-start(f32[4,128,128]{1,2,0:T(8,128)S(1)} %custom-call.34) | copy-start | bytes 786436
  459.4 1.0 copy-start.5
  548.4 52.6 %copy-start.8 = (f32[4,128,128]{1,2,0:T(8,128)S(1)}, f32[4,128,128]{1,2,0:T(8,128)}, u32[]{:S(2)}) copy-start(f32[4,128,128]{1,2,0:T(8,128)} %copy-done.7) | copy-start | bytes 786436
  598.5 3.5 copy-start.4
  605.3 4.2 copy-start.3
Sparse Core Ops, SparseCore 0:
  29.6 68.3 all-reduce.7
  133.9 169.4 all-reduce.5
where the time goes:
time: 641 us; the launch traced here: 635 us
  other arithmetic  258 us (40%)
  waiting for transfers between devices  238 us (37%)
  matrix products  86.7 us (14%)
  local copies, waits for them, and re-layouts  32.3 us (5%)
  between operations  19.4 us (3%)
    psum x1, waiting for transfers between devices, shards(): lax.psum((part_one, part_two, small_one, small_two), 'grp')  170 us
    another operation x5, other arithmetic, solve_lower(): return lax.linalg.triangular_solve(lower, right, left_side=True, lower=True)  80.2 us
    another operation x15, other arithmetic, shards(): jnp.linalg.cholesky(corner_two - jnp.dot(cross.T, cross, precision=highest))  79.6 us
    another operation x14, other arithmetic, shards(): lower_one = jnp.linalg.cholesky(corner_one[:, :width])  79 us
    psum x1, waiting for transfers between devices, from_root(): return lax.psum(kept, axis)  68 us
    another operation x21, matrix products, solve_lower(): return lax.linalg.triangular_solve(lower, right, left_side=True, lower=True)  29.1 us
    another operation x27, local copies, waits for them, and re-layouts, solve_lower(): return lax.linalg.triangular_solve(lower, right, left_side=True, lower=True)  19.9 us
    concatenate x1, other arithmetic, shards(): jnp.concatenate([factor_rows, new_rows], 0).reshape(-1, npanel * width)  15.4 us
  transfers between devices with their start and end apart: 2, of which 2 were waited for; matrix products, arithmetic and copies ran while one was open for 0% of the time, Pallas kernels for 0%

commit v1 on v0

--- a/solution.py
+++ b/solution.py
@@ -4,9 +4,14 @@
 from jax.sharding import PartitionSpec as P
 
 
+def lead_stages_all_on_mesh(load, along_axis):
+    all_rows = lax.all_gather(load, axis_name=along_axis)
+    return jnp.sum(all_rows, 0)
+
+
 def from_root(value, axis, source):
     kept = jnp.where(lax.axis_index(axis) == source, value, 0).astype(value.dtype)
-    return lax.psum(kept, axis)
+    return lead_stages_all_on_mesh(kept, axis)
 
 
 def solve_lower(lower, right):

time: 641 us -> 678 us (1.058)
  waiting for transfers between devices: 238 us -> 252 us
  matrix products: 86.7 us -> 99.5 us
  other arithmetic: 258 us -> 268 us
    all_gather x0 -> x2, waiting for transfers between devices: none -> 83.6 us  [lead_stages_all_on_mesh(): all_rows = lax.all_gather(load, axis_name=along_axis)]
    psum x1 -> x0, waiting for transfers between devices: 68 us -> none  [from_root(): return lax.psum(kept, axis)]
    dot_general x1, matrix products: 13.7 us -> 24.7 us  [shards(): jnp.dot(second.T, local, precision=highest, preferred_element_type=jnp.fl...]
    reduce_sum x0 -> x2, other arithmetic: none -> 9.9 us  [lead_stages_all_on_mesh(): return jnp.sum(all_rows, 0)]
  transfers between devices with their start and end apart: 2 -> 3, of which waited for: 2 -> 3; matrix products, arithmetic and copies ran while one was open for 0% -> 4% of each run, Pallas kernels for 0% -> 0%
where the time goes in v1:
time: 678 us; the launch traced here: 671 us
  other arithmetic  268 us (40%)
  waiting for transfers between devices  252 us (37%)
  matrix products  99.5 us (15%)
  local copies, waits for them, and re-layouts  32.6 us (5%)
  between operations  18.8 us (3%)
    psum x1, waiting for transfers between devices, shards(): lax.psum((part_one, part_two, small_one, small_two), 'grp')  168 us
    all_gather x2, waiting for transfers between devices, lead_stages_all_on_mesh(): all_rows = lax.all_gather(load, axis_name=along_axis)  83.6 us
    another operation x5, other arithmetic, solve_lower(): return lax.linalg.triangular_solve(lower, right, left_side=True, lower=True)  80.4 us
    another operation x15, other arithmetic, shards(): jnp.linalg.cholesky(corner_two - jnp.dot(cross.T, cross, precision=highest))  79.4 us
    another operation x14, other arithmetic, shards(): lower_one = jnp.linalg.cholesky(corner_one[:, :width])  78.9 us
    another operation x21, matrix products, solve_lower(): return lax.linalg.triangular_solve(lower, right, left_side=True, lower=True)  29.1 us
    dot_general x1, matrix products, shards(): jnp.dot(second.T, local, precision=highest, preferred_element_type=jnp.fl...  24.7 us
    another operation x27, local copies, waits for them, and re-layouts, solve_lower(): return lax.linalg.triangular_solve(lower, right, left_side=True, lower=True)  20 us
  transfers between devices with their start and end apart: 3, of which 3 were waited for; matrix products, arithmetic and copies ran while one was open for 4% of the time, Pallas kernels for 0%

profile of v1, /device:TPU:1, one launch (start us, length us, event | category | flops | bytes accessed | tf_op | source)
XLA Modules:
  0.0 671.5 jit_solution(352612033404210304)
XLA Ops:
  6.5 15.4 %maximum_reduce_fusion = f32[576,4,512]{2,1,0:T(4,128)S(1)} fusion(f32[512,4,1,512]{3,2,1,0:T(1,128)} %param.6, f32[64,4,1,512]{3,2,1,0:T(1,128)} %param.5), kind=kLoop, calls=%fused_computation.12 | loop fusion | flops 1179648 | bytes 9437184 | tf_op jit(solution)/shard_map/concatenate | solution.py:26
  22.0 4.4 copy.11
  26.4 3.1 slice_select_fusion.1
  30.3 57.2 %all-gather.7.cloned.1.call-done = f32[4608,512]{1,0:T(8,128)} async-done(((f32[576,512]{1,0:T(8,128)}), f32[4608,512]{1,0:T(8,128)}) %all-gather.7.cloned.1.call-update) | async-done | bytes 9437200 | tf_op jit(solution)/shard_map/all_gather | solution.py:8
  87.5 4.9 reduce_sum.19
  92.5 24.7 %fusion.115 = f32[512,2048]{1,0:T(8,128)} fusion(f32[576,512]{1,0:T(8,128)S(1)} %reduce_sum.19, f32[576,2048]{1,0:T(8,128)} %bitcast.123), kind=kOutput, calls=%fused_computation.189 | convolution fusion | flops 7247757312 | bytes 10092544 | tf_op jit(solution)/shard_map/dot_general | solution.py:31
  117.2 26.4 %all-gather.5.cloned.1.call-done = f32[4608,512]{1,0:T(8,128)} async-done(((f32[576,512]{1,0:T(8,128)}), f32[4608,512]{1,0:T(8,128)}) %all-gather.5.cloned.1.call-update) | async-done | bytes 9437200 | tf_op jit(solution)/shard_map/all_gather | solution.py:8
  143.6 4.9 reduce_sum.18
  148.6 6.5 fusion.29
  155.1 13.6 %fusion.113 = f32[512,2048]{1,0:T(8,128)} fusion(f32[576,512]{1,0:T(8,128)S(1)} %reduce_sum.18, f32[576,2048]{1,0:T(8,128)} %bitcast.124), kind=kOutput, calls=%fused_computation.187 | convolution fusion | flops 7247757312 | bytes 10092544 | tf_op jit(solution)/shard_map/dot_general | solution.py:30
  168.7 3.8 fusion.114
  172.5 167.9 %all-reduce.4.cloned.1.call-done = (f32[512,2048]{1,0:T(8,128)}, f32[512,2048]{1,0:T(8,128)}, f32[512,1024]{0,1:T(8,128)}, f32[512,512]{0,1:T(8,128)}) async-done(((f32[512,2048]{1,0:T(8,128)}, f32[512,2048]{1,0:T(8,128)}, f32[512,1024]{0,1:T(8,128)}, f32[512,512]{0,1:T(8,128)}), (f32[512,2048]{1,0:T(8,128)}, f32[512,2048]{1,0:T(8,128)}, f32[512,1024]{0,1:T(8,128)}, ...) | async-done | bytes 11534352 | tf_op jit(solution)/shard_map/psum | solution.py:35
  340.4 2.5 slice.184
  342.9 1.6 copy.4
  344.7 1.1 copy-done.4
  345.8 11.7 %cholesky.286 = f32[128,128]{1,0:T(8,128)S(1)} custom-call(f32[128,128]{1,0:T(8,128)S(1)} %cholesky.426), custom_call_target="Cholesky" | custom-call | tf_op jit(solution)/shard_map/jit(cholesky)/cholesky | solution.py:38
  357.5 9.8 %custom-call.31 = f32[1,128,128]{1,2,0:T(8,128)S(1)} custom-call(f32[1,128,128]{2,1,0:T(8,128)S(1)} %get-tuple-element.76), custom_call_target="InvertDiagBlocksLowerTriangular" | custom-call | tf_op jit(solution)/shard_map/jit(cholesky)/cholesky | solution.py:38
  367.5 1.2 constant_dynamic-update-slice_fusion.1
  368.7 1.3 convolution_subtract_fusion.9
  370.0 11.9 %cholesky.305 = f32[128,128]{1,0:T(8,128)S(1)} custom-call(f32[128,128]{1,0:T(8,128)S(1)} %cholesky.430), custom_call_target="Cholesky" | custom-call | tf_op jit(solution)/shard_map/jit(cholesky)/cholesky | solution.py:38
  381.9 9.8 %custom-call.32 = f32[1,128,128]{1,2,0:T(8,128)S(1)} custom-call(f32[1,128,128]{2,1,0:T(8,128)S(1)} %get-tuple-element.73), custom_call_target="InvertDiagBlocksLowerTriangular" | custom-call | tf_op jit(solution)/shard_map/jit(cholesky)/cholesky | solution.py:38
  392.0 1.3 convolution_subtract_fusion.11
  393.3 11.7 %cholesky.326 = f32[128,128]{1,0:T(8,128)S(1)} custom-call(f32[128,128]{1,0:T(8,128)S(1)} %cholesky.435), custom_call_target="Cholesky" | custom-call | tf_op jit(solution)/shard_map/jit(cholesky)/cholesky | solution.py:38
  405.7 9.8 %custom-call.33 = f32[1,128,128]{1,2,0:T(8,128)S(1)} custom-call(f32[1,128,128]{2,1,0:T(8,128)S(1)} %get-tuple-element.70), custom_call_target="InvertDiagBlocksLowerTriangular" | custom-call | tf_op jit(solution)/shard_map/jit(cholesky)/cholesky | solution.py:38
  415.7 1.2 convolution_subtract_fusion.13
  417.0 12.1 %cholesky.343 = f32[128,128]{1,0:T(8,128)S(1)} custom-call(f32[128,128]{1,0:T(8,128)S(1)} %convolution_subtract_fusion.13), custom_call_target="Cholesky" | custom-call | tf_op jit(solution)/shard_map/jit(cholesky)/cholesky | solution.py:38
  432.8 1.2 select_select_fusion.1
  434.0 11.9 %while.5 = (s32[]{:T(128)}, f32[512,512]{1,0:T(8,128)}, s32[4,2]{0,1:T(2,128)S(1)}, f32[4,128,128]{2,1,0:T(8,128)S(1)}, s32[]{:T(128)}) while((s32[]{:T(128)}, f32[512,512]{1,0:T(8,128)}, s32[4,2]{0,1:T(2,128)S(1)}, f32[4,128,128]{2,1,0:T(8,128)S(1)}, s32[]{:T(128)}) %tuple.55), condition=%wide.while_cond, body=%wide.while_body.sunk | while | flops 2 | bytes 131181 | solution.py:18
  434.7 2.3 bitcast_dynamic-update-slice_fusion.4
  437.6 2.3 bitcast_dynamic-update-slice_fusion.4
  440.6 2.3 bitcast_dynamic-update-slice_fusion.4
  443.6 2.2 bitcast_dynamic-update-slice_fusion.4
  445.9 39.3 %custom-call.34 = f32[4,128,128]{1,2,0:T(8,128)S(1)} custom-call(f32[4,128,128]{2,1,0:T(8,128)S(1)} %get-tuple-element.29), custom_call_target="InvertDiagBlocksLowerTriangular" | custom-call | tf_op jit(solution)/shard_map/triangular_solve/custom-call.3 | solution.py:18
  485.6 1.4 convolution_subtract_fusion.6
  487.5 1.9 convolution_subtract_fusion.5
  489.8 2.4 convolution_subtract_fusion.7
  492.7 3.1 convolution_subtract_fusion.4
  497.3 11.7 %cholesky.358 = f32[128,128]{1,0:T(8,128)S(1)} custom-call(f32[128,128]{1,0:T(8,128)S(1)} %cholesky.439), custom_call_target="Cholesky" | custom-call | tf_op jit(solution)/shard_map/jit(cholesky)/cholesky | solution.py:40
  509.2 10.0 %custom-call.35 = f32[1,128,128]{1,2,0:T(8,128)S(1)} custom-call(f32[1,128,128]{2,1,0:T(8,128)S(1)} %get-tuple-element.66), custom_call_target="InvertDiagBlocksLowerTriangular" | custom-call | tf_op jit(solution)/shard_map/jit(cholesky)/cholesky | solution.py:40
  519.2 1.2 constant_dynamic-update-slice_fusion
  520.4 1.3 convolution_subtract_fusion.8
  521.7 11.7 %cholesky.377 = f32[128,128]{1,0:T(8,128)S(1)} custom-call(f32[128,128]{1,0:T(8,128)S(1)} %cholesky.443), custom_call_target="Cholesky" | custom-call | tf_op jit(solution)/shard_map/jit(cholesky)/cholesky | solution.py:40
  534.7 9.8 %custom-call.36 = f32[1,128,128]{1,2,0:T(8,128)S(1)} custom-call(f32[1,128,128]{2,1,0:T(8,128)S(1)} %get-tuple-element.63), custom_call_target="InvertDiagBlocksLowerTriangular" | custom-call | tf_op jit(solution)/shard_map/jit(cholesky)/cholesky | solution.py:40
  544.8 1.3 convolution_subtract_fusion.10
  546.1 11.7 %cholesky.398 = f32[128,128]{1,0:T(8,128)S(1)} custom-call(f32[128,128]{1,0:T(8,128)S(1)} %cholesky.448), custom_call_target="Cholesky" | custom-call | tf_op jit(solution)/shard_map/jit(cholesky)/cholesky | solution.py:40
  558.6 10.0 %custom-call.37 = f32[1,128,128]{1,2,0:T(8,128)S(1)} custom-call(f32[1,128,128]{2,1,0:T(8,128)S(1)} %get-tuple-element.60), custom_call_target="InvertDiagBlocksLowerTriangular" | custom-call | tf_op jit(solution)/shard_map/jit(cholesky)/cholesky | solution.py:40
  568.8 1.2 convolution_subtract_fusion.12
  570.0 11.7 %cholesky.415 = f32[128,128]{1,0:T(8,128)S(1)} custom-call(f32[128,128]{1,0:T(8,128)S(1)} %convolution_subtract_fusion.12), custom_call_target="Cholesky" | custom-call | tf_op jit(solution)/shard_map/jit(cholesky)/cholesky | solution.py:40
  585.2 8.3 %while.6 = (s32[]{:T(128)}, f32[512,512]{1,0:T(8,128)S(1)}, s32[4,2]{0,1:T(2,128)S(1)}, f32[4,128,128]{2,1,0:T(8,128)S(1)}, s32[]{:T(128)}) while((s32[]{:T(128)}, f32[512,512]{1,0:T(8,128)S(1)}, s32[4,2]{0,1:T(2,128)S(1)}, f32[4,128,128]{2,1,0:T(8,128)S(1)}, s32[]{:T(128)}) %tuple.68), condition=%wide.while_cond.clone, body=%wide.while_body.clone.sunk | while | flops 2 | bytes 131181 | solution.py:18
  585.8 1.4 bitcast_dynamic-update-slice_fusion.5
  587.9 1.4 bitcast_dynamic-update-slice_fusion.5
  590.0 1.4 bitcast_dynamic-update-slice_fusion.5
  592.1 1.4 bitcast_dynamic-update-slice_fusion.5
  593.5 39.7 %custom-call.38 = f32[4,128,128]{1,2,0:T(8,128)S(1)} custom-call(f32[4,128,128]{2,1,0:T(8,128)S(1)} %get-tuple-element.30), custom_call_target="InvertDiagBlocksLowerTriangular" | custom-call | tf_op jit(solution)/shard_map/triangular_solve/custom-call.3 | solution.py:18
  633.2 2.3 fusion.41
  635.5 2.4 convolution_subtract_fusion.3
  639.0 2.2 convolution_subtract_fusion.1
  641.2 1.1 fusion.97
  642.3 3.1 fusion.26
  646.5 7.7 %fusion.20 = f32[512,2048]{1,0:T(8,128)S(1)} fusion(f32[512,2048]{1,0:T(8,128)S(1)} %copy-done.1, f32[128,2048]{1,0:T(8,128)S(1)} %fusion.99, f32[128,2048]{1,0:T(8,128)S(1)} %fusion.97, f32[128,2048]{1,0:T(8,128)S(1)} %fusion.95, f32[128,2048]{1,0:T(8,128)S(1)} %fusion.41, f32[128,512]{1,0:T(8,128)S(1)} %fusion.98, f32[128,512]{1,0:T(8,128)S(1)} %fusion.96, ...), kind=kOutput, calls=%fused_computation.33 | convolution fusion | flops 6447431680 | bytes 13631488 | tf_op jit(solution)/shard_map/dot_general | solution.py:42
  657.3 1.3 convolution_subtract_fusion
  658.6 1.1 fusion.81
  659.7 2.0 fusion.23
  663.3 1.4 reshape.50
  (81 shorter events, 22.7 us)
Async XLA Ops:
  6.5 81.0 %all-gather.7.cloned.1.call-start = ((), (), s32[]{:S(2)}) async-start(), calls=%async_computation.1 | async-start | bytes 10616832 | tf_op jit(solution)/shard_map/all_gather | solution.py:8
  29.5 114.1 %all-gather.5.cloned.1.call-start = ((), (), s32[]{:S(2)}) async-start(), calls=%async_computation | async-start | bytes 10616832 | tf_op jit(solution)/shard_map/all_gather | solution.py:8
  30.2 310.1 %all-reduce.4.cloned.1.call-start = ((), (), s32[]{:S(2)}) async-start(), calls=%async_computation.2 | async-start | bytes 23068672 | tf_op jit(solution)/shard_map/psum | solution.py:35
  340.4 4.1 copy-start
  344.7 1.1 copy-start.4
  485.2 7.5 %copy-start.5 = (f32[4,128,128]{1,2,0:T(8,128)}, f32[4,128,128]{1,2,0:T(8,128)S(1)}, u32[]{:S(2)}) copy-start(f32[4,128,128]{1,2,0:T(8,128)S(1)} %custom-call.34) | copy-start | bytes 786436
  496.3 1.0 copy-start.3
  585.1 52.8 %copy-start.6 = (f32[4,128,128]{1,2,0:T(8,128)S(1)}, f32[4,128,128]{1,2,0:T(8,128)}, u32[]{:S(2)}) copy-start(f32[4,128,128]{1,2,0:T(8,128)} %copy-done.5) | copy-start | bytes 786436
  635.5 3.5 copy-start.2
  642.3 4.2 copy-start.1
Sparse Core Ops, SparseCore 0:
  29.6 57.8 all-gather.6
  89.2 54.3 all-gather.4
  172.6 167.7 all-reduce.3
